TPU v7x, 256 devices: a whole 4x4x8 slice. The times are simulated.
256 devices in a mesh: seq: 16 (over x, y), tp: 16 (over z, core).
Axes of the slice: x: 4, y: 4, z: 8, core: 2. Of those that a mesh axis runs over, the one named last changes fastest.
Arguments:
- query: bfloat16 [16384, 8192], P('seq', 'tp'), may hold values from -6 to 6
- key_in: bfloat16 [16384, 8192], P('seq', 'tp'), may hold values from -6 to 6
- value: bfloat16 [16384, 8192], P('seq', 'tp'), may hold values from -6 to 6
- gate: bfloat16 [16384, 8192], P('seq', 'tp'), may hold values from -8 to 8
- kv_start: float32 [64, 128, 128], P('tp'), may hold values from -240 to 240
- norm_gain: float32 [8192], P('tp'), may hold values from 0.5 to 2
- w_out: bfloat16 [8192, 6144], P('tp'), may hold values from -0.0625 to 0.0625
Outputs:
- mixed: bfloat16 [16384, 6144], P(('seq', 'tp'))
All inputs are finite; a program needn't handle non-finite values.
Results may differ from a plain program's by a relative error of at most 0.019.
Values may be sent and summed in bfloat16 or wider, within the bound.
No kernel may reach another device: no remote copies, remote signals or barrier semaphores. Data moves between devices by JAX's collectives and lax.ppermute only.
A program may use at most 128 MiB of HBM per device.

v0:
```python
import jax
import jax.numpy as jnp
from jax import lax
from jax.sharding import PartitionSpec as P

HD = 128


def per_device(query, key_in, value, gate, kv_start, norm_gain, w_out):
    rows = query.shape[0]
    heads = query.shape[1] // HD
    block = min(512, rows)
    count = rows // block
    highest = lax.Precision.HIGHEST
    qa = (
        jax.nn.silu(query.astype(jnp.float32)).astype(jnp.bfloat16).reshape(count, block, heads, HD)
    )
    ka = (
        jax.nn.silu(key_in.astype(jnp.float32))
        .astype(jnp.bfloat16)
        .reshape(count, block, heads, HD)
    )
    va = value.reshape(count, block, heads, HD)
    block_states = jnp.einsum("nthd,nthe->nhde", ka, va, preferred_element_type=jnp.float32)
    own_total = jnp.sum(block_states, axis=0)
    local_before = jnp.cumsum(block_states, axis=0) - block_states
    gathered = lax.all_gather(
        own_total[None].astype(jnp.bfloat16), "seq", axis=0, tiled=True
    ).astype(jnp.float32)
    position = lax.axis_index("seq")
    below = (jnp.arange(gathered.shape[0]) < position).astype(jnp.float32)
    prior = jnp.sum(gathered * below[:, None, None, None], axis=0)
    states = local_before + (kv_start + prior)[None]
    q_float = qa.astype(jnp.float32)
    inter = jnp.einsum("nthd,nhde->nthe", q_float, states, precision=highest)
    scores = jnp.einsum("nthd,nshd->nhts", qa, ka, preferred_element_type=jnp.float32)
    causal = jnp.arange(block)[:, None] >= jnp.arange(block)[None, :]
    scores = jnp.where(causal[None, None], scores, jnp.float32(0.0))
    intra = jnp.einsum("nhts,nshe->nthe", scores, va.astype(jnp.float32), precision=highest)
    heads_out = (inter + intra).reshape(rows, heads, HD)
    scale = lax.rsqrt(jnp.mean(heads_out * heads_out, axis=-1, keepdims=True) + 1e-05)
    normed = (heads_out * scale).reshape(rows, heads * HD)
    attn = (normed * norm_gain[None, :] * jax.nn.sigmoid(gate.astype(jnp.float32))).astype(
        jnp.bfloat16
    )
    return lax.psum_scatter(
        jnp.dot(attn, w_out, preferred_element_type=jnp.float32).astype(jnp.bfloat16),
        "tp",
        scatter_dimension=0,
        tiled=True,
    )


def solution(mesh):
    in_specs = (
        P("seq", "tp"),
        P("seq", "tp"),
        P("seq", "tp"),
        P("seq", "tp"),
        P("tp", None, None),
        P("tp"),
        P("tp", None),
    )
    out_specs = P(("seq", "tp"), None)
    return jax.shard_map(
        per_device, mesh=mesh, in_specs=in_specs, out_specs=out_specs, check_vma=False
    )
```

profile of v0, /device:TPU:2, one launch (start us, length us, event | category | flops | bytes accessed | tf_op | source)
XLA Modules:
  0.0 170.8 jit_solution(4474242960137433406)
XLA Ops:
  6.5 0.0 all-gather.3.cloned.1.call-start
  6.5 1.8 %fusion.8 = bf16[1024,512]{1,0:T(8,128)(2,1)S(1)} fusion(bf16[1024,512]{1,0:T(8,128)(2,1)} %param.8), kind=kLoop, calls=%fused_computation.14 | loop fusion | flops 3145728 | bytes 2097152 | tf_op jit(solution)/shard_map/convert_element_type | solution.py:20
  8.4 0.3 reshape.60
  8.7 1.3 reshape.61
  10.0 0.7 copy.33
  10.7 0.0 copy-start.3
  10.7 2.0 %fusion.28 = (bf16[4,128,128]{2,1,0:T(8,128)(2,1)}, f32[2,4,128,128]{3,2,1,0:T(8,128)}) fusion(bf16[2,512,4,128]{1,3,2,0:T(8,128)(2,1)S(1)} %copy.33, bf16[2,512,4,128]{3,2,1,0:T(4,128)(2,1)S(1)} %reshape.60), kind=kOutput, calls=%fused_computation.40 | convolution fusion | flops 134283264 | bytes 2752512 | tf_op jit(solution)/shard_map/nthd,nthe->nhde/dot_general | solution.py:24
  12.7 0.0 all-gather.3.cloned.1.call-update
  12.7 0.0 reduce-scatter.2.cloned.1.call-start
  12.7 0.0 copy-done.3
  12.7 1.6 fusion.12
  14.3 1.3 reshape.62
  15.7 0.1 iota_compare_fusion
  15.8 1.3 fusion.22
  17.0 6.7 %fusion = f32[2,4,512,128]{2,3,1,0:T(8,128)} fusion(bf16[2,512,4,128]{1,3,2,0:T(8,128)(2,1)S(1)} %copy.33, f32[2,4,512,512]{3,2,1,0:T(8,128)S(1)} %fusion.22, pred[512,512]{1,0:T(8,128)(4,1)S(1)} %iota_compare_fusion), kind=kOutput, calls=%fused_computation.1 | convolution fusion | flops 3223322624 | bytes 11796480 | tf_op jit(solution)/shard_map/nhts,nshe->nthe/dot_general | solution.py:39
  23.7 0.0 copy-start.4
  23.7 0.0 copy-start.1
  23.7 41.7 %all-gather.3.cloned.1.call-done = bf16[64,128,128]{2,1,0:T(8,128)(2,1)} async-done(((bf16[4,128,128]{2,1,0:T(8,128)(2,1)}), bf16[64,128,128]{2,1,0:T(8,128)(2,1)}) %all-gather.3.cloned.1.call-update) | async-done | bytes 2097168 | tf_op jit(solution)/shard_map/all_gather | solution.py:27
  65.4 0.0 copy-start
  65.4 2.2 %fusion.2 = f32[4,128,128]{2,1,0:T(8,128)S(1)} fusion(bf16[16,4,128,128]{3,2,1,0:T(8,128)(2,1)} %bitcast.27, f32[16]{0:T(128)S(1)} %compare_convert_fusion), kind=kLoop, calls=%fused_computation.4 | loop fusion | flops 3080192 | bytes 2359360 | tf_op jit(solution)/shard_map/reduce_sum | solution.py:32
  67.6 0.0 copy-done.4
  67.7 0.0 copy-done.1
  67.7 0.1 fusion.16
  67.9 0.0 copy-done
  67.9 1.3 multiply_reduce_fusion
  69.2 0.2 copy.35
  69.4 1.9 %copy.34 = f32[2,512,4,128]{3,2,1,0:T(4,128)} copy(f32[2,512,4,128]{1,3,2,0:T(8,128)S(1)} %get-tuple-element.8) | data formatting | bytes 4194304 | tf_op jit(solution)/shard_map/add | solution.py:40
  71.3 0.0 copy-start.2
  71.3 0.0 copy-start.5
  71.3 1.2 mul.46
  72.5 0.4 copy-done.2
  72.8 0.0 copy-done.5
  72.8 11.9 %convolution_convert_fusion = bf16[1024,6144]{1,0:T(8,128)(2,1)} fusion(bf16[512,6144]{1,0:T(8,128)(2,1)} %param.13, f32[128,8,4,128]{3,2,1,0:T(4,128)S(1)} %bitcast.28, f32[128,8,4,128]{3,2,1,0:T(4,128)S(1)} %bitcast.29, bf16[1024,512]{1,0:T(8,128)(2,1)} %param.10, f32[512]{0:T(512)S(1)} %copy-done.5), kind=kOutput, calls=%fused_computation | convolution fusion | flops 6452936704 | bytes 24119296 | tf_op jit(solution)/shard_map/dot_general | solution.py:47
  84.7 0.0 reduce-scatter.2.cloned.1.call-update
  84.8 79.2 %reduce-scatter.2.cloned.1.call-done = bf16[64,6144]{1,0:T(8,128)(2,1)} async-done(((bf16[1024,6144]{1,0:T(8,128)(2,1)}), bf16[64,6144]{1,0:T(8,128)(2,1)}) %reduce-scatter.2.cloned.1.call-update) | async-done | bytes 786448 | tf_op jit(solution)/shard_map/reduce_scatter | solution.py:46
  (3 shorter events, 0.1 us)
Async XLA Ops:
  6.5 58.8 %all-gather.3.cloned.1.call-start = ((), (), s32[]{:S(2)}) async-start(), calls=%async_computation.2 | async-start | bytes 2228224 | tf_op jit(solution)/shard_map/all_gather | solution.py:27
  10.7 2.1 %copy-start.3 = (bf16[1024,512]{1,0:T(8,128)(2,1)S(1)}, bf16[1024,512]{1,0:T(8,128)(2,1)}, u32[]{:S(2)}) copy-start(bf16[1024,512]{1,0:T(8,128)(2,1)} %param.7) | copy-start | bytes 3145732
  12.7 151.3 %reduce-scatter.2.cloned.1.call-start = ((), (), s32[]{:S(2)}) async-start(), calls=%async_computation.1 | async-start | bytes 13369344 | tf_op jit(solution)/shard_map/reduce_scatter | solution.py:46
  23.7 43.9 %copy-start.4 = (f32[4,128,128]{2,1,0:T(8,128)S(1)}, f32[4,128,128]{2,1,0:T(8,128)}, u32[]{:S(2)}) copy-start(f32[4,128,128]{2,1,0:T(8,128)} %param.11) | copy-start | bytes 786436
  23.7 44.0 %copy-start.1 = (f32[2,4,128,128]{3,2,1,0:T(8,128)S(1)}, f32[2,4,128,128]{3,2,1,0:T(8,128)}, u32[]{:S(2)}) copy-start(f32[2,4,128,128]{3,2,1,0:T(8,128)} %get-tuple-element.6) | copy-start | bytes 1572868
  65.4 2.5 %copy-start = (f32[2,4,512,128]{2,3,1,0:T(8,128)S(1)}, f32[2,4,512,128]{2,3,1,0:T(8,128)}, u32[]{:S(2)}) copy-start(f32[2,4,512,128]{2,3,1,0:T(8,128)} %fusion) | copy-start | bytes 6291460
  71.3 1.6 copy-start.2
  71.3 1.6 copy-start.5
Sparse Core Ops, SparseCore 0:
  12.8 52.5 all-gather.2
  84.9 79.0 reduce-scatter.1
where the time goes:
time: 171 us
  waiting for transfers between devices  121 us (71%)
  matrix products  23 us (13%)
  between operations  13.6 us (8%)
  local copies, waits for them, and re-layouts  7.34 us (4%)
  other arithmetic  5.92 us (3%)
    reduce_scatter x1, waiting for transfers between devices, per_device(): lax.psum_scatter(jnp.dot(attn, w_out, preferred_element_type=jnp.float32)...  79.2 us
    all_gather x1, waiting for transfers between devices, per_device(): lax.all_gather(own_total[None].astype(jnp.bfloat16), 'seq', axis=0, tiled...  41.7 us
    dot_general x1, matrix products, per_device(): jnp.dot(attn, w_out, preferred_element_type=jnp.float32)  11.9 us
    dot_general x1, matrix products, per_device(): jnp.einsum('nhts,nshe->nthe', scores, va.astype(jnp.float32), precision=h...  6.66 us
  transfers between devices with their start and end apart: 2, of which 2 were waited for; matrix products, arithmetic and copies ran while one was open for 6% of the time, Pallas kernels for 0%

commit v1 on v0

--- a/solution.py
+++ b/solution.py
@@ -24,8 +24,11 @@
     block_states = jnp.einsum("nthd,nthe->nhde", ka, va, preferred_element_type=jnp.float32)
     own_total = jnp.sum(block_states, axis=0)
     local_before = jnp.cumsum(block_states, axis=0) - block_states
-    gathered = lax.all_gather(
-        own_total[None].astype(jnp.bfloat16), "seq", axis=0, tiled=True
+    gathered = jnp.concatenate(
+        lax.all_to_all(
+            jnp.stack([own_total[None].astype(jnp.bfloat16)] * lax.axis_size("seq")), "seq", 0, 0
+        ),
+        axis=0,
     ).astype(jnp.float32)
     position = lax.axis_index("seq")
     below = (jnp.arange(gathered.shape[0]) < position).astype(jnp.float32)

time: 171 us -> 157 us (0.918)
  waiting for transfers between devices: 121 us -> 97.9 us
  starting transfers between devices: 0.04 us -> 7.83 us
  local copies, waits for them, and re-layouts: 7.34 us -> 9.14 us
    all_gather x1 -> x0, waiting for transfers between devices: 41.7 us -> none  [per_device(): lax.all_gather(own_total[None].astype(jnp.bfloat16), 'seq', axis=0, tiled...]
    all_to_all x0 -> x1, waiting for transfers between devices: none -> 16 us  [per_device(): lax.all_to_all(jnp.stack([own_total[None].astype(jnp.bfloat16)] * lax.axi...]
    all_to_all x0 -> x1, starting transfers between devices: none -> 7.61 us  [per_device(): lax.all_to_all(jnp.stack([own_total[None].astype(jnp.bfloat16)] * lax.axi...]
    reduce_scatter x1, waiting for transfers between devices: 79.2 us -> 81.8 us  [per_device(): lax.psum_scatter(jnp.dot(attn, w_out, preferred_element_type=jnp.float32)...]
    another operation x0 -> x1, local copies, waits for them, and re-layouts: none -> 1.8 us  [per_device(): jnp.stack([own_total[None].astype(jnp.bfloat16)] * lax.axis_size('seq'))]
  transfers between devices with their start and end apart: 2 -> 2, of which waited for: 2 -> 2; matrix products, arithmetic and copies ran while one was open for 6% -> 7% of each run, Pallas kernels for 0% -> 0%
where the time goes in v1:
time: 157 us
  waiting for transfers between devices  97.9 us (62%)
  matrix products  22.4 us (14%)
  between operations  13.6 us (9%)
  local copies, waits for them, and re-layouts  9.14 us (6%)
  starting transfers between devices  7.83 us (5%)
  other arithmetic  5.91 us (4%)
    reduce_scatter x1, waiting for transfers between devices, per_device(): lax.psum_scatter(jnp.dot(attn, w_out, preferred_element_type=jnp.float32)...  81.8 us
    all_to_all x1, waiting for transfers between devices, per_device(): lax.all_to_all(jnp.stack([own_total[None].astype(jnp.bfloat16)] * lax.axi...  16 us
    dot_general x1, matrix products, per_device(): jnp.dot(attn, w_out, preferred_element_type=jnp.float32)  11.9 us
    all_to_all x1, starting transfers between devices, per_device(): lax.all_to_all(jnp.stack([own_total[None].astype(jnp.bfloat16)] * lax.axi...  7.61 us
    dot_general x1, matrix products, per_device(): jnp.einsum('nhts,nshe->nthe', scores, va.astype(jnp.float32), precision=h...  6.7 us
  transfers between devices with their start and end apart: 2, of which 2 were waited for; matrix products, arithmetic and copies ran while one was open for 7% of the time, Pallas kernels for 0%

profile of v1, /device:TPU:2, one launch (start us, length us, event | category | flops | bytes accessed | tf_op | source)
XLA Modules:
  0.0 156.7 jit_solution(2376800612872693562)
XLA Ops:
  6.5 1.8 %fusion.8 = bf16[1024,512]{1,0:T(8,128)(2,1)S(1)} fusion(bf16[1024,512]{1,0:T(8,128)(2,1)} %param.8), kind=kLoop, calls=%fused_computation.14 | loop fusion | flops 3145728 | bytes 2097152 | tf_op jit(solution)/shard_map/convert_element_type | solution.py:20
  8.4 0.3 reshape.62
  8.7 1.3 reshape.63
  10.0 0.7 copy.51
  10.7 1.3 fusion.28
  12.0 1.8 %stack.2 = bf16[16,1,4,128,128]{4,3,2,1,0:T(8,128)(2,1)} broadcast(bf16[4,128,128]{2,1,0:T(8,128)(2,1)S(1)} %get-tuple-element.5), dimensions={2,3,4} | broadcast | bytes 2228224 | tf_op jit(solution)/shard_map/stack | solution.py:29
  13.8 0.0 copy-start.3
  13.8 7.6 %all-to-all-start = ((bf16[16,1,4,128,128]{4,3,2,1,0:T(8,128)(2,1)}), bf16[16,1,4,128,128]{4,3,2,1,0:T(8,128)(2,1)}, u32[]{:S(2)}, u32[]{:S(2)}) async-start(bf16[16,1,4,128,128]{4,3,2,1,0:T(8,128)(2,1)} %stack.2), calls=%async_computation | async-start | bytes 4194304 | tf_op jit(solution)/shard_map/all_to_all | solution.py:28
  21.4 0.2 reduce-scatter.2.cloned.1.call-start
  21.6 0.0 copy-done.3
  21.6 1.6 %fusion.12 = bf16[1024,512]{1,0:T(8,128)(2,1)} fusion(bf16[1024,512]{1,0:T(8,128)(2,1)S(1)} %copy-done.3), kind=kLoop, calls=%fused_computation.18 | loop fusion | flops 3145728 | bytes 2097152 | tf_op jit(solution)/shard_map/convert_element_type | solution.py:16
  23.2 1.3 reshape.64
  24.6 0.1 iota_compare_fusion
  24.7 1.3 fusion.22
  25.9 6.7 %fusion = f32[2,4,512,128]{2,3,1,0:T(8,128)} fusion(bf16[2,512,4,128]{1,3,2,0:T(8,128)(2,1)S(1)} %copy.51, f32[2,4,512,512]{3,2,1,0:T(8,128)S(1)} %fusion.22, pred[512,512]{1,0:T(8,128)(4,1)S(1)} %iota_compare_fusion), kind=kOutput, calls=%fused_computation.1 | convolution fusion | flops 3223322624 | bytes 11796480 | tf_op jit(solution)/shard_map/nhts,nshe->nthe/dot_general | solution.py:42
  32.6 0.0 copy-start.4
  32.6 0.0 copy-start.1
  32.6 16.0 %all-to-all-done = bf16[16,1,4,128,128]{4,3,2,1,0:T(8,128)(2,1)} async-done(((bf16[16,1,4,128,128]{4,3,2,1,0:T(8,128)(2,1)}), bf16[16,1,4,128,128]{4,3,2,1,0:T(8,128)(2,1)}, u32[]{:S(2)}, u32[]{:S(2)}) %all-to-all-start) | async-done | bytes 2097184 | tf_op jit(solution)/shard_map/all_to_all | solution.py:28
  48.7 0.0 copy-start
  48.7 2.2 %fusion.2 = f32[4,128,128]{2,1,0:T(8,128)S(1)} fusion(bf16[16,1,4,128,128]{4,3,2,1,0:T(8,128)(2,1)} %all-to-all-done, f32[16]{0:T(128)S(1)} %compare_convert_fusion), kind=kLoop, calls=%fused_computation.4 | loop fusion | flops 3080192 | bytes 2359360 | tf_op jit(solution)/shard_map/reduce_sum | solution.py:35
  50.9 0.0 copy-done.4
  51.0 0.0 copy-done.1
  51.0 0.1 fusion.16
  51.1 0.0 copy-done
  51.1 1.3 multiply_reduce_fusion
  52.4 0.2 copy.53
  52.7 1.9 %copy.52 = f32[2,512,4,128]{3,2,1,0:T(4,128)} copy(f32[2,512,4,128]{1,3,2,0:T(8,128)S(1)} %get-tuple-element.8) | data formatting | bytes 4194304 | tf_op jit(solution)/shard_map/add | solution.py:43
  54.5 0.0 copy-start.2
  54.5 0.0 copy-start.5
  54.5 1.2 mul.46
  55.8 0.4 copy-done.2
  56.1 0.0 copy-done.5
  56.1 11.9 %convolution_convert_fusion = bf16[1024,6144]{1,0:T(8,128)(2,1)} fusion(bf16[512,6144]{1,0:T(8,128)(2,1)} %param.13, f32[128,8,4,128]{3,2,1,0:T(4,128)S(1)} %bitcast.28, f32[128,8,4,128]{3,2,1,0:T(4,128)S(1)} %bitcast.29, bf16[1024,512]{1,0:T(8,128)(2,1)} %param.10, f32[512]{0:T(512)S(1)} %copy-done.5), kind=kOutput, calls=%fused_computation | convolution fusion | flops 6452936704 | bytes 24119296 | tf_op jit(solution)/shard_map/dot_general | solution.py:50
  68.0 0.0 reduce-scatter.2.cloned.1.call-update
  68.1 81.8 %reduce-scatter.2.cloned.1.call-done = bf16[64,6144]{1,0:T(8,128)(2,1)} async-done(((bf16[1024,6144]{1,0:T(8,128)(2,1)}), bf16[64,6144]{1,0:T(8,128)(2,1)}) %reduce-scatter.2.cloned.1.call-update) | async-done | bytes 786448 | tf_op jit(solution)/shard_map/reduce_scatter | solution.py:49
  (3 shorter events, 0.1 us)
Async XLA Ops:
  13.8 7.8 %copy-start.3 = (bf16[1024,512]{1,0:T(8,128)(2,1)S(1)}, bf16[1024,512]{1,0:T(8,128)(2,1)}, u32[]{:S(2)}) copy-start(bf16[1024,512]{1,0:T(8,128)(2,1)} %param.7) | copy-start | bytes 3145732
  13.8 34.9 %all-to-all-start = ((bf16[16,1,4,128,128]{4,3,2,1,0:T(8,128)(2,1)}), bf16[16,1,4,128,128]{4,3,2,1,0:T(8,128)(2,1)}, u32[]{:S(2)}, u32[]{:S(2)}) async-start(bf16[16,1,4,128,128]{4,3,2,1,0:T(8,128)(2,1)} %stack.2), calls=%async_computation | async-start | bytes 4194304 | tf_op jit(solution)/shard_map/all_to_all | solution.py:28
  21.4 128.5 %reduce-scatter.2.cloned.1.call-start = ((), (), s32[]{:S(2)}) async-start(), calls=%async_computation.2 | async-start | bytes 13369344 | tf_op jit(solution)/shard_map/reduce_scatter | solution.py:49
  32.6 18.3 %copy-start.4 = (f32[4,128,128]{2,1,0:T(8,128)S(1)}, f32[4,128,128]{2,1,0:T(8,128)}, u32[]{:S(2)}) copy-start(f32[4,128,128]{2,1,0:T(8,128)} %param.11) | copy-start | bytes 786436
  32.6 18.3 %copy-start.1 = (f32[2,4,128,128]{3,2,1,0:T(8,128)S(1)}, f32[2,4,128,128]{3,2,1,0:T(8,128)}, u32[]{:S(2)}) copy-start(f32[2,4,128,128]{3,2,1,0:T(8,128)} %get-tuple-element.6) | copy-start | bytes 1572868
  48.7 2.5 %copy-start = (f32[2,4,512,128]{2,3,1,0:T(8,128)S(1)}, f32[2,4,512,128]{2,3,1,0:T(8,128)}, u32[]{:S(2)}) copy-start(f32[2,4,512,128]{2,3,1,0:T(8,128)} %fusion) | copy-start | bytes 6291460
  54.5 1.6 %copy-start.2 = (f32[2,512,4,128]{3,2,1,0:T(4,128)S(1)}, f32[2,512,4,128]{3,2,1,0:T(4,128)}, u32[]{:S(2)}) copy-start(f32[2,512,4,128]{3,2,1,0:T(4,128)} %copy.52) | copy-start | bytes 6291460
  54.5 1.6 %copy-start.5 = (f32[512]{0:T(512)S(1)}, f32[512]{0:T(512)}, u32[]{:S(2)}) copy-start(f32[512]{0:T(512)} %param.12) | copy-start | bytes 6148
Sparse Core Ops, SparseCore 0:
  68.2 81.6 reduce-scatter.1
